TPU v7x, 32 devices: a whole 2x2x4 slice. The times are simulated.
32 devices in a mesh: shard: 8 (over z, x), tensor: 4 (over y, core).
Axes of the slice: x: 2, y: 2, z: 4, core: 2. Of those that a mesh axis runs over, the one named last changes fastest.
Arguments:
- wide_weight: bfloat16 [4, 4096, 4096], P(None, 'shard', 'tensor'), may hold values from -6 to 6
- wide_grad: bfloat16 [4, 4096, 4096], P(None, 'shard', 'tensor'), may hold values from -6 to 6
- wide_first: float32 [4, 4096, 256], P(None, ('shard', 'tensor')), may hold values from -4 to 4
- wide_second: float32 [4, 4096, 256], P(None, ('shard', 'tensor')), may hold values from 0.001 to 0.1
- wide_basis: bfloat16 [4, 4096, 256], P(None, 'tensor'), may hold values from -0.09375 to 0.09375
- narrow_weight: bfloat16 [4, 1024, 4096], P(None, 'shard', 'tensor'), may hold values from -6 to 6
- narrow_grad: bfloat16 [4, 1024, 4096], P(None, 'shard', 'tensor'), may hold values from -6 to 6
- narrow_first: float32 [4, 1024, 256], P(None, ('shard', 'tensor')), may hold values from -4 to 4
- narrow_second: float32 [4, 1024, 256], P(None, ('shard', 'tensor')), may hold values from 0.001 to 0.1
- narrow_basis: bfloat16 [4, 4096, 256], P(None, 'tensor'), may hold values from -0.09375 to 0.09375
- vocab_weight: bfloat16 [2, 32000, 4096], P(None, 'shard', 'tensor'), may hold values from -6 to 6
- vocab_grad: bfloat16 [2, 32000, 4096], P(None, 'shard', 'tensor'), may hold values from -6 to 6
- vocab_first: float32 [2, 32000, 256], P(None, ('shard', 'tensor')), may hold values from -4 to 4
- vocab_second: float32 [2, 32000, 256], P(None, ('shard', 'tensor')), may hold values from 0.001 to 0.1
- vocab_basis: bfloat16 [2, 4096, 256], P(None, 'tensor'), may hold values from -0.09375 to 0.09375
Outputs:
- wide_weight_new: bfloat16 [4, 4096, 4096], P(None, 'shard', 'tensor')
- wide_first_new: float32 [4, 4096, 256], P(None, ('shard', 'tensor'))
- wide_second_new: float32 [4, 4096, 256], P(None, ('shard', 'tensor'))
- narrow_weight_new: bfloat16 [4, 1024, 4096], P(None, 'shard', 'tensor')
- narrow_first_new: float32 [4, 1024, 256], P(None, ('shard', 'tensor'))
- narrow_second_new: float32 [4, 1024, 256], P(None, ('shard', 'tensor'))
- vocab_weight_new: bfloat16 [2, 32000, 4096], P(None, 'shard', 'tensor')
- vocab_first_new: float32 [2, 32000, 256], P(None, ('shard', 'tensor'))
- vocab_second_new: float32 [2, 32000, 256], P(None, ('shard', 'tensor'))
All inputs are finite; a program needn't handle non-finite values.
Results may differ from a plain program's by a relative error of at most 0.01.
Values may be sent and summed in bfloat16 or wider, within the bound.
No kernel may reach another device: no remote copies, remote signals or barrier semaphores. Data moves between devices by JAX's collectives and lax.ppermute only.
A program may use at most 192 MiB of HBM per device.

v0:
```python
import functools
import jax
import jax.numpy as jnp
from jax import lax
from jax.sharding import PartitionSpec as P

NS_ITERS = 3
HIGHEST = lax.Precision.HIGHEST


def local_gram(polish):
    return jnp.einsum("sdk,sdl->skl", polish, polish, precision=HIGHEST)


def polish_small(back, gram):
    trace = jnp.einsum("skk->s", gram)
    scale = 1.0 / jnp.sqrt(trace + 1e-06)
    small = gram * (scale * scale)[:, None, None]
    rank = gram.shape[1]
    eye = jnp.eye(rank, dtype=jnp.float32)[None, :, :]
    factor = jnp.broadcast_to(eye, gram.shape)
    for step in range(NS_ITERS):
        square = jnp.einsum("skl,slm->skm", small, small, precision=HIGHEST)
        turn = 3.4445 * eye - 4.775 * small + 2.0315 * square
        factor = jnp.einsum("skl,slm->skm", factor, turn, precision=HIGHEST)
        if step + 1 < NS_ITERS:
            small = jnp.einsum(
                "skl,slm->skm",
                turn,
                jnp.einsum("skl,slm->skm", small, turn, precision=HIGHEST),
                precision=HIGHEST,
            )
    return jnp.einsum("sdk,skl->sdl", back * scale[:, None, None], factor, precision=HIGHEST)


def adam_moments(first, second, projected):
    first_new = 0.9 * first + 0.1 * projected
    second_new = 0.999 * second + 0.001 * projected * projected
    direction = first_new / (1.0 - 0.9**10) / (jnp.sqrt(second_new / (1.0 - 0.999**10)) + 1e-08)
    return (first_new, second_new, direction.astype(jnp.bfloat16))


def split_rows(flat, shapes):
    parts = []
    offset = 0
    for shape in shapes:
        size = 1
        for dim in shape:
            size *= dim
        parts.append(flat[..., offset : offset + size].reshape(flat.shape[:-1] + shape))
        offset += size
    return parts


def per_device(
    tensor_size,
    wide_weight,
    wide_grad,
    wide_first,
    wide_second,
    wide_basis,
    narrow_weight,
    narrow_grad,
    narrow_first,
    narrow_second,
    narrow_basis,
    vocab_weight,
    vocab_grad,
    vocab_first,
    vocab_second,
    vocab_basis,
):
    weights = (wide_weight, narrow_weight, vocab_weight)
    grads = (wide_grad, narrow_grad, vocab_grad)
    firsts = (wide_first, narrow_first, vocab_first)
    seconds = (wide_second, narrow_second, vocab_second)
    olds = (wide_basis, narrow_basis, vocab_basis)
    counts = [grad.shape[0] for grad in grads]
    sketch_terms = [
        jnp.einsum("smc,scr->smr", grad, old, preferred_element_type=jnp.float32).astype(
            jnp.bfloat16
        )
        for grad, old in zip(grads, olds)
    ]
    sketches = lax.psum(tuple(sketch_terms), "tensor")
    back_terms = [
        jnp.einsum("smc,smr->scr", grad, sketch, preferred_element_type=jnp.float32)
        for grad, sketch in zip(grads, sketches)
    ]
    back_all = jnp.concatenate(back_terms, axis=0).astype(jnp.bfloat16)
    backs = lax.psum_scatter(back_all, "shard", scatter_dimension=1, tiled=True).astype(jnp.float32)
    grams = lax.psum(local_gram(backs), ("shard", "tensor"))
    rounded = polish_small(backs, grams).astype(jnp.bfloat16)
    basis_all = lax.all_gather(rounded, "shard", axis=1, tiled=True)
    bases = []
    offset = 0
    for count in counts:
        bases.append(basis_all[offset : offset + count])
        offset += count
    proj_parts = []
    row_shapes = []
    for grad, basis in zip(grads, bases):
        count, rows, cols = grad.shape
        split = grad.reshape(count, tensor_size, rows // tensor_size, cols)
        proj = jnp.einsum("sjmc,scr->jsmr", split, basis, preferred_element_type=jnp.float32)
        row_shapes.append((count, rows // tensor_size, basis.shape[2]))
        proj_parts.append(proj.reshape(tensor_size, -1, basis.shape[2]).astype(jnp.bfloat16))
    proj_all = jnp.concatenate(proj_parts, axis=1)
    proj_mine = lax.psum_scatter(proj_all, "tensor", scatter_dimension=0, tiled=True).reshape(-1)
    projected = [part.astype(jnp.float32) for part in split_rows(proj_mine, row_shapes)]
    results = [
        adam_moments(first, second, proj) for first, second, proj in zip(firsts, seconds, projected)
    ]
    dir_all = jnp.concatenate([result[2].reshape(-1) for result in results])
    dir_gathered = lax.all_gather(dir_all, "tensor", axis=0, tiled=False)
    directions = split_rows(dir_gathered, row_shapes)
    outputs = []
    for weight, direction, basis, result in zip(weights, directions, bases, results):
        count, rows, cols = weight.shape
        update = jnp.einsum("jsmr,scr->sjmc", direction, basis, preferred_element_type=jnp.float32)
        update = update.reshape(count, rows, cols)
        weight_new = (0.99 * weight.astype(jnp.float32) - 2.0 * update).astype(jnp.bfloat16)
        outputs.append((weight_new, result[0], result[1]))
    return (
        outputs[0][0],
        outputs[0][1],
        outputs[0][2],
        outputs[1][0],
        outputs[1][1],
        outputs[1][2],
        outputs[2][0],
        outputs[2][1],
        outputs[2][2],
    )


def solution(mesh):
    in_specs = (
        P(None, "shard", "tensor"),
        P(None, "shard", "tensor"),
        P(None, ("shard", "tensor"), None),
        P(None, ("shard", "tensor"), None),
        P(None, "tensor", None),
        P(None, "shard", "tensor"),
        P(None, "shard", "tensor"),
        P(None, ("shard", "tensor"), None),
        P(None, ("shard", "tensor"), None),
        P(None, "tensor", None),
        P(None, "shard", "tensor"),
        P(None, "shard", "tensor"),
        P(None, ("shard", "tensor"), None),
        P(None, ("shard", "tensor"), None),
        P(None, "tensor", None),
    )
    out_specs = (
        P(None, "shard", "tensor"),
        P(None, ("shard", "tensor"), None),
        P(None, ("shard", "tensor"), None),
        P(None, "shard", "tensor"),
        P(None, ("shard", "tensor"), None),
        P(None, ("shard", "tensor"), None),
        P(None, "shard", "tensor"),
        P(None, ("shard", "tensor"), None),
        P(None, ("shard", "tensor"), None),
    )
    return jax.shard_map(
        functools.partial(per_device, mesh.shape["tensor"]),
        mesh=mesh,
        in_specs=in_specs,
        out_specs=out_specs,
        check_vma=False,
    )
```

profile of v0, /device:TPU:0, one launch (start us, length us, event | category | flops | bytes accessed | tf_op | source)
XLA Modules:
  0.0 731.9 jit_solution(9271300986264332978)
XLA Ops:
  10.4 4.5 convolution_convert_fusion.2
  14.9 12.1 %convolution_convert_fusion = bf16[2,4000,256]{2,1,0:T(8,128)(2,1)} fusion(bf16[2,4000,1024]{2,1,0:T(8,128)(2,1)} %param.26, bf16[2,1024,256]{2,1,0:T(8,128)(2,1)S(1)} %copy-done.16), kind=kOutput, calls=%fused_computation.5 | convolution fusion | flops 4196352000 | bytes 21528576 | tf_op jit(solution)/shard_map/smc,scr->smr/dot_general | solution.py:80
  27.4 108.1 %all-reduce.6.cloned.1.call-done = (bf16[2,4000,256]{2,1,0:T(8,128)(2,1)}, bf16[4,128,256]{2,1,0:T(8,128)(2,1)}, bf16[4,512,256]{2,1,0:T(8,128)(2,1)}) async-done(((bf16[2,4000,256]{2,1,0:T(8,128)(2,1)}, bf16[4,128,256]{2,1,0:T(8,128)(2,1)}, bf16[4,512,256]{2,1,0:T(8,128)(2,1)}), (bf16[2,4000,256]{2,1,0:T(8,128)(2,1)}, bf16[4,128,256]{2,1,0:T(8,128)(2,1)}, ...) | async-done | bytes 5406736 | tf_op jit(solution)/shard_map/psum | solution.py:85
  135.5 11.6 %fusion.32 = bf16[2,1024,256]{1,2,0:T(8,128)(2,1)S(1)} fusion(bf16[2,4000,256]{2,1,0:T(8,128)(2,1)} %get-tuple-element.9, bf16[2,4000,1024]{2,1,0:T(8,128)(2,1)} %param.26), kind=kOutput, calls=%fused_computation.55 | convolution fusion | flops 4194828288 | bytes 21528576 | tf_op jit(solution)/shard_map/smc,smr->scr/dot_general | solution.py:87
  152.5 11.6 %copy.51 = bf16[10,1024,256]{2,0,1:T(8,128)(2,1)} copy(bf16[10,1024,256]{1,2,0:T(8,128)(2,1)} %pad_maximum_fusion.1) | data formatting | bytes 10485760
  164.1 9.2 %copy.53 = bf16[128,8,10,256]{3,1,2,0:T(8,128)(2,1)} copy(bf16[128,8,10,256]{3,2,1,0:T(8,128)(2,1)} %bitcast.110) | data formatting | bytes 10485760
  173.4 103.0 %reduce-scatter.7.cloned.1.call-done = bf16[128,2560]{1,0:T(8,128)(2,1)} async-done(((bf16[1024,2560]{1,0:T(8,128)(2,1)}), bf16[128,2560]{1,0:T(8,128)(2,1)}) %reduce-scatter.7.cloned.1.call-update) | async-done | bytes 655376
  281.4 137.8 %all-reduce.4.cloned.1.call-done = f32[10,256,256]{2,1,0:T(8,128)} async-done(((f32[10,256,256]{2,1,0:T(8,128)}), f32[10,256,256]{2,1,0:T(8,128)}) %all-reduce.4.cloned.1.call-update) | async-done | bytes 2621456 | tf_op jit(solution)/shard_map/psum | solution.py:92
  424.9 3.5 fusion.15
  428.3 3.3 fusion.14
  434.8 3.3 fusion.9
  440.8 3.3 fusion.10
  444.1 3.5 fusion.8
  453.5 3.3 convolution_convert_fusion.3
  456.8 84.8 %all-gather.4.cloned.1.call-done = bf16[10,1024,256]{2,1,0:T(8,128)(2,1)} async-done(((bf16[10,128,256]{2,1,0:T(8,128)(2,1)}), bf16[10,1024,256]{2,1,0:T(8,128)(2,1)}) %all-gather.4.cloned.1.call-update) | async-done | bytes 5242896 | tf_op jit(solution)/shard_map/all_gather | solution.py:94
  547.4 8.3 %convert_bitcast_fusion = bf16[4,2,1000,256]{3,2,0,1:T(8,128)(2,1)S(1)} fusion(bf16[2,4,1000,1024]{3,2,1,0:T(8,128)(2,1)} %bitcast.134, bf16[10,1024,256]{2,1,0:T(8,128)(2,1)} %all-gather.4.cloned.1.call-done), kind=kOutput, calls=%fused_computation.10 | convolution fusion | flops 4196352000 | bytes 21528576 | tf_op jit(solution)/shard_map/sjmc,scr->jsmr/dot_general | solution.py:105
  559.3 50.4 %reduce-scatter.5.cloned.1.call-done = bf16[1,2640,256]{2,1,0:T(8,128)(2,1)} async-done(((bf16[4,2640,256]{2,1,0:T(8,128)(2,1)}), bf16[1,2640,256]{2,1,0:T(8,128)(2,1)}) %reduce-scatter.5.cloned.1.call-update) | async-done | bytes 1351696 | tf_op jit(solution)/shard_map/reduce_scatter | solution.py:109
  615.2 3.5 divide_convert_fusion
  621.0 41.5 %all-gather.6.cloned.1.call-done = bf16[2703360]{0:T(1024)(128)(2,1)} async-done(((bf16[675840]{0:T(1024)(128)(2,1)}), bf16[2703360]{0:T(1024)(128)(2,1)}) %all-gather.6.cloned.1.call-update) | async-done | bytes 5406736 | tf_op jit(solution)/shard_map/all_gather | solution.py:115
  662.5 6.9 reshape.109
  676.2 4.7 broadcast_multiply_fusion
  680.9 7.2 fusion.1
  688.1 14.3 %convolution_multiply_fusion = f32[2,4,1000,1024]{3,2,1,0:T(8,128)} fusion(bf16[4,2,1000,256]{3,2,1,0:T(8,128)(2,1)S(1)} %bitcast.109, bf16[10,1024,256]{2,1,0:T(8,128)(2,1)} %all-gather.4.cloned.1.call-done), kind=kOutput, calls=%fused_computation.2 | convolution fusion | flops 4202496000 | bytes 37912576 | tf_op jit(solution)/shard_map/jsmr,scr->sjmc/dot_general | solution.py:120
  702.3 22.5 %fusion = bf16[2,4000,1024]{2,1,0:T(8,128)(2,1)} fusion(f32[2,4,1000,1024]{3,2,1,0:T(8,128)} %convolution_multiply_fusion, bf16[2,4000,1024]{2,1,0:T(8,128)(2,1)} %param.25), kind=kLoop, calls=%fused_computation.1 | loop fusion | flops 32768000 | bytes 65536000 | tf_op jit(solution)/shard_map/convert_element_type | solution.py:122
  (95 shorter events, 55.2 us)
Async XLA Ops:
  7.2 3.3 copy-start
  7.2 128.3 %all-reduce.6.cloned.1.call-start = ((), (), s32[]{:S(2)}) async-start(), calls=%async_computation.7 | async-start | bytes 10813440 | tf_op jit(solution)/shard_map/psum | solution.py:85
  10.4 4.5 copy-start.16
  27.0 249.4 %reduce-scatter.7.cloned.1.call-start = ((), (), s32[]{:S(2)}) async-start(), calls=%async_computation.6 | async-start | bytes 5898240
  135.5 11.6 %copy-start.5 = (bf16[4,128,1024]{2,1,0:T(8,128)(2,1)S(1)}, bf16[4,128,1024]{2,1,0:T(8,128)(2,1)}, u32[]{:S(2)}) copy-start(bf16[4,128,1024]{2,1,0:T(8,128)(2,1)} %param.21) | copy-start | bytes 3145732
  135.5 11.6 %copy-start.13 = (bf16[4,128,256]{2,1,0:T(8,128)(2,1)S(1)}, bf16[4,128,256]{2,1,0:T(8,128)(2,1)}, u32[]{:S(2)}) copy-start(bf16[4,128,256]{2,1,0:T(8,128)(2,1)} %get-tuple-element.10) | copy-start | bytes 786436
  135.5 12.4 %copy-start.3 = (bf16[4,512,1024]{2,1,0:T(8,128)(2,1)S(1)}, bf16[4,512,1024]{2,1,0:T(8,128)(2,1)}, u32[]{:S(2)}) copy-start(bf16[4,512,1024]{2,1,0:T(8,128)(2,1)} %param.16) | copy-start | bytes 12582916
  173.4 245.9 %all-reduce.4.cloned.1.call-start = ((), (), s32[]{:S(2)}) async-start(), calls=%async_computation.2 | async-start | bytes 5242880 | tf_op jit(solution)/shard_map/psum | solution.py:92
  280.8 260.9 %all-gather.4.cloned.1.call-start = ((), (), s32[]{:S(2)}) async-start(), calls=%async_computation.3 | async-start | bytes 5898240 | tf_op jit(solution)/shard_map/all_gather | solution.py:94
  419.3 2.5 copy-start.2
  456.8 152.9 %reduce-scatter.5.cloned.1.call-start = ((), (), s32[]{:S(2)}) async-start(), calls=%async_computation.4 | async-start | bytes 6758400 | tf_op jit(solution)/shard_map/reduce_scatter | solution.py:109
  541.7 2.8 copy-start.4
  558.8 51.7 %copy-start.14 = (f32[4,32,256]{2,1,0:T(8,128)S(1)}, f32[4,32,256]{2,1,0:T(8,128)}, u32[]{:S(2)}) copy-start(f32[4,32,256]{2,1,0:T(8,128)} %param.22) | copy-start | bytes 393220
  558.8 51.7 %copy-start.15 = (f32[4,32,256]{2,1,0:T(8,128)S(1)}, f32[4,32,256]{2,1,0:T(8,128)}, u32[]{:S(2)}) copy-start(f32[4,32,256]{2,1,0:T(8,128)} %param.23) | copy-start | bytes 393220
  558.8 53.5 %copy-start.11 = (f32[4,128,256]{2,1,0:T(8,128)S(1)}, f32[4,128,256]{2,1,0:T(8,128)}, u32[]{:S(2)}) copy-start(f32[4,128,256]{2,1,0:T(8,128)} %param.17) | copy-start | bytes 1572868
  558.8 53.5 %copy-start.12 = (f32[4,128,256]{2,1,0:T(8,128)S(1)}, f32[4,128,256]{2,1,0:T(8,128)}, u32[]{:S(2)}) copy-start(f32[4,128,256]{2,1,0:T(8,128)} %param.18) | copy-start | bytes 1572868
  558.9 103.6 %all-gather.6.cloned.1.call-start = ((), (), s32[]{:S(2)}) async-start(), calls=%async_computation.5 | async-start | bytes 6758400 | tf_op jit(solution)/shard_map/all_gather | solution.py:115
  612.3 2.3 copy-start.8
  612.3 2.9 copy-start.9
  669.4 2.3 slice-start.2
  669.4 4.1 slice-start.3
  671.7 2.0 slice-start.4
  676.2 4.7 copy-start.6
  702.3 22.5 %copy-start.1 = (bf16[4,1024,256]{2,1,0:T(8,128)(2,1)S(1)}, bf16[4,1024,256]{2,1,0:T(8,128)(2,1)}, u32[]{:S(2)}) copy-start(bf16[4,1024,256]{2,1,0:T(8,128)(2,1)} %param.19) | copy-start | bytes 6291460
  (5 other events, 6.7 us)
Sparse Core Ops, SparseCore 0:
  27.2 108.2 all-reduce.5
  173.5 102.8 reduce-scatter.6
  283.3 135.8 all-reduce.3
  456.9 84.6 all-gather.3
  559.0 50.6 reduce-scatter.4
  621.1 41.3 all-gather.5
where the time goes:
time: 737 us; the launch traced here: 732 us
  waiting for transfers between devices  526 us (71%)
  matrix products  103 us (14%)
  other arithmetic  45.9 us (6%)
  local copies, waits for them, and re-layouts  40.7 us (6%)
  between operations  14.7 us (2%)
    psum x1, waiting for transfers between devices, per_device(): grams = lax.psum(local_gram(backs), ('shard', 'tensor'))  138 us
    psum x1, waiting for transfers between devices, per_device(): sketches = lax.psum(tuple(sketch_terms), 'tensor')  108 us
    unnamed x7, waiting for transfers between devices  103 us
    all_gather x1, waiting for transfers between devices, per_device(): basis_all = lax.all_gather(rounded, 'shard', axis=1, tiled=True)  84.8 us
    reduce_scatter x1, waiting for transfers between devices, per_device(): lax.psum_scatter(proj_all, 'tensor', scatter_dimension=0, tiled=True)  50.4 us
    all_gather x1, waiting for transfers between devices, per_device(): dir_gathered = lax.all_gather(dir_all, 'tensor', axis=0, tiled=False)  41.5 us
    convert_element_type x3, other arithmetic, per_device(): (0.99 * weight.astype(jnp.float32) - 2.0 * update).astype(jnp.bfloat16)  31.1 us
    unnamed x48, local copies, waits for them, and re-layouts  28.2 us
  transfers between devices with their start and end apart: 6, of which 6 were waited for; matrix products, arithmetic and copies ran while one was open for 0% of the time, Pallas kernels for 0%

commit v1 on v0

--- a/solution.py
+++ b/solution.py
@@ -91,7 +91,14 @@
     backs = lax.psum_scatter(back_all, "shard", scatter_dimension=1, tiled=True).astype(jnp.float32)
     grams = lax.psum(local_gram(backs), ("shard", "tensor"))
     rounded = polish_small(backs, grams).astype(jnp.bfloat16)
-    basis_all = lax.all_gather(rounded, "shard", axis=1, tiled=True)
+    devices = lax.axis_size("shard")
+    forward = [(i, (i + 1) % devices) for i in range(devices)]
+    pieces = [rounded]
+    for hop in range(1, devices):
+        pieces = [lax.ppermute(pieces[0], "shard", forward), *pieces]
+    whole = jnp.concatenate(pieces, axis=1)
+    shift = (lax.axis_index("shard") + 1) * pieces[-1].shape[1]
+    basis_all = jnp.roll(whole, shift, axis=1)
     bases = []
     offset = 0
     for count in counts:

time: 737 us -> 772 us (1.047)
  waiting for transfers between devices: 526 us -> 547 us
  local copies, waits for them, and re-layouts: 40.7 us -> 53.5 us
    ppermute x0 -> x7, waiting for transfers between devices: none -> 106 us  [per_device(): pieces = [lax.ppermute(pieces[0], 'shard', forward), *pieces]]
    all_gather x1 -> x0, waiting for transfers between devices: 84.8 us -> none  [per_device(): basis_all = lax.all_gather(rounded, 'shard', axis=1, tiled=True)]
    unnamed x48 -> x77, local copies, waits for them, and re-layouts: 28.2 us -> 41.3 us
    unnamed x7 -> x6, waiting for transfers between devices: 103 us -> 103 us
  transfers between devices with their start and end apart: 6 -> 12, of which waited for: 6 -> 12; matrix products, arithmetic and copies ran while one was open for 0% -> 0% of each run, Pallas kernels for 0% -> 0%
where the time goes in v1:
time: 772 us; the launch traced here: 766 us
  waiting for transfers between devices  547 us (71%)
  matrix products  102 us (13%)
  local copies, waits for them, and re-layouts  53.5 us (7%)
  other arithmetic  45.9 us (6%)
  between operations  14.6 us (2%)
    psum x1, waiting for transfers between devices, per_device(): grams = lax.psum(local_gram(backs), ('shard', 'tensor'))  138 us
    psum x1, waiting for transfers between devices, per_device(): sketches = lax.psum(tuple(sketch_terms), 'tensor')  108 us
    ppermute x7, waiting for transfers between devices, per_device(): pieces = [lax.ppermute(pieces[0], 'shard', forward), *pieces]  106 us
    unnamed x6, waiting for transfers between devices  103 us
    reduce_scatter x1, waiting for transfers between devices, per_device(): lax.psum_scatter(proj_all, 'tensor', scatter_dimension=0, tiled=True)  50.3 us
    all_gather x1, waiting for transfers between devices, per_device(): dir_gathered = lax.all_gather(dir_all, 'tensor', axis=0, tiled=False)  41.5 us
    unnamed x77, local copies, waits for them, and re-layouts  41.3 us
    convert_element_type x3, other arithmetic, per_device(): (0.99 * weight.astype(jnp.float32) - 2.0 * update).astype(jnp.bfloat16)  31.1 us
  transfers between devices with their start and end apart: 12, of which 12 were waited for; matrix products, arithmetic and copies ran while one was open for 0% of the time, Pallas kernels for 0%

profile of v1, /device:TPU:0, one launch (start us, length us, event | category | flops | bytes accessed | tf_op | source)
XLA Modules:
  0.0 766.3 jit_solution(5557348728912901871)
XLA Ops:
  10.4 4.5 convolution_convert_fusion.2
  14.9 12.1 %convolution_convert_fusion = bf16[2,4000,256]{2,1,0:T(8,128)(2,1)} fusion(bf16[2,4000,1024]{2,1,0:T(8,128)(2,1)} %param.26, bf16[2,1024,256]{2,1,0:T(8,128)(2,1)S(1)} %copy-done.25), kind=kOutput, calls=%fused_computation.5 | convolution fusion | flops 4196352000 | bytes 21528576 | tf_op jit(solution)/shard_map/smc,scr->smr/dot_general | solution.py:80
  27.4 108.1 %all-reduce.6.cloned.1.call-done = (bf16[2,4000,256]{2,1,0:T(8,128)(2,1)}, bf16[4,128,256]{2,1,0:T(8,128)(2,1)}, bf16[4,512,256]{2,1,0:T(8,128)(2,1)}) async-done(((bf16[2,4000,256]{2,1,0:T(8,128)(2,1)}, bf16[4,128,256]{2,1,0:T(8,128)(2,1)}, bf16[4,512,256]{2,1,0:T(8,128)(2,1)}), (bf16[2,4000,256]{2,1,0:T(8,128)(2,1)}, bf16[4,128,256]{2,1,0:T(8,128)(2,1)}, ...) | async-done | bytes 5406736 | tf_op jit(solution)/shard_map/psum | solution.py:85
  135.5 11.6 %fusion.32 = bf16[2,1024,256]{1,2,0:T(8,128)(2,1)S(1)} fusion(bf16[2,4000,256]{2,1,0:T(8,128)(2,1)} %get-tuple-element.9, bf16[2,4000,1024]{2,1,0:T(8,128)(2,1)} %param.26), kind=kOutput, calls=%fused_computation.55 | convolution fusion | flops 4194828288 | bytes 21528576 | tf_op jit(solution)/shard_map/smc,smr->scr/dot_general | solution.py:87
  152.6 11.6 %copy.51 = bf16[10,1024,256]{2,0,1:T(8,128)(2,1)} copy(bf16[10,1024,256]{1,2,0:T(8,128)(2,1)} %pad_maximum_fusion.1) | data formatting | bytes 10485760
  164.2 9.2 %copy.53 = bf16[128,8,10,256]{3,1,2,0:T(8,128)(2,1)} copy(bf16[128,8,10,256]{3,2,1,0:T(8,128)(2,1)} %bitcast.110) | data formatting | bytes 10485760
  173.5 103.0 %reduce-scatter.7.cloned.1.call-done = bf16[128,2560]{1,0:T(8,128)(2,1)} async-done(((bf16[1024,2560]{1,0:T(8,128)(2,1)}), bf16[128,2560]{1,0:T(8,128)(2,1)}) %reduce-scatter.7.cloned.1.call-update) | async-done | bytes 655376
  281.5 137.8 %all-reduce.4.cloned.1.call-done = f32[10,256,256]{2,1,0:T(8,128)} async-done(((f32[10,256,256]{2,1,0:T(8,128)}), f32[10,256,256]{2,1,0:T(8,128)}) %all-reduce.4.cloned.1.call-update) | async-done | bytes 2621456 | tf_op jit(solution)/shard_map/psum | solution.py:92
  457.4 16.3 %collective-permute-done = bf16[10,128,256]{2,1,0:T(8,128)(2,1)S(1)} collective-permute-done((bf16[10,128,256]{2,1,0:T(8,128)(2,1)S(1)}, bf16[10,128,256]{2,1,0:T(8,128)(2,1)S(1)}, u32[]{:S(2)}, u32[]{:S(2)}) %collective-permute-start) | collective-permute-done | bytes 655392 | tf_op jit(solution)/shard_map/ppermute | solution.py:98
  473.7 16.7 %collective-permute-done.1 = bf16[10,128,256]{2,1,0:T(8,128)(2,1)S(1)} collective-permute-done((bf16[10,128,256]{2,1,0:T(8,128)(2,1)S(1)}, bf16[10,128,256]{2,1,0:T(8,128)(2,1)S(1)}, u32[]{:S(2)}, u32[]{:S(2)}) %collective-permute-start.1) | collective-permute-done | bytes 655392 | tf_op jit(solution)/shard_map/ppermute | solution.py:98
  491.2 15.8 %collective-permute-done.2 = bf16[10,128,256]{2,1,0:T(8,128)(2,1)S(1)} collective-permute-done((bf16[10,128,256]{2,1,0:T(8,128)(2,1)S(1)}, bf16[10,128,256]{2,1,0:T(8,128)(2,1)S(1)}, u32[]{:S(2)}, u32[]{:S(2)}) %collective-permute-start.2) | collective-permute-done | bytes 655392 | tf_op jit(solution)/shard_map/ppermute | solution.py:98
  507.8 14.8 %collective-permute-done.3 = bf16[10,128,256]{2,1,0:T(8,128)(2,1)S(1)} collective-permute-done((bf16[10,128,256]{2,1,0:T(8,128)(2,1)S(1)}, bf16[10,128,256]{2,1,0:T(8,128)(2,1)S(1)}, u32[]{:S(2)}, u32[]{:S(2)}) %collective-permute-start.3) | collective-permute-done | bytes 655392 | tf_op jit(solution)/shard_map/ppermute | solution.py:98
  523.5 14.1 %collective-permute-done.4 = bf16[10,128,256]{2,1,0:T(8,128)(2,1)S(1)} collective-permute-done((bf16[10,128,256]{2,1,0:T(8,128)(2,1)S(1)}, bf16[10,128,256]{2,1,0:T(8,128)(2,1)S(1)}, u32[]{:S(2)}, u32[]{:S(2)}) %collective-permute-start.4) | collective-permute-done | bytes 655392 | tf_op jit(solution)/shard_map/ppermute | solution.py:98
  538.4 14.9 %collective-permute-done.5 = bf16[10,128,256]{2,1,0:T(8,128)(2,1)} collective-permute-done((bf16[10,128,256]{2,1,0:T(8,128)(2,1)S(1)}, bf16[10,128,256]{2,1,0:T(8,128)(2,1)}, u32[]{:S(2)}, u32[]{:S(2)}) %collective-permute-start.5) | collective-permute-done | bytes 655392 | tf_op jit(solution)/shard_map/ppermute | solution.py:98
  553.6 13.5 %collective-permute-done.6 = bf16[10,128,256]{2,1,0:T(8,128)(2,1)} collective-permute-done((bf16[10,128,256]{2,1,0:T(8,128)(2,1)}, bf16[10,128,256]{2,1,0:T(8,128)(2,1)}, u32[]{:S(2)}, u32[]{:S(2)}) %collective-permute-start.6) | collective-permute-done | bytes 655392 | tf_op jit(solution)/shard_map/ppermute | solution.py:98
  572.9 4.5 copy-done.4
  578.8 8.3 %convert_bitcast_fusion = bf16[4,2,1000,256]{3,2,0,1:T(8,128)(2,1)S(1)} fusion(bf16[2,4,1000,1024]{3,2,1,0:T(8,128)(2,1)} %bitcast.132, bf16[10,2048,256]{2,1,0:T(8,128)(2,1)} %copy-done.7, s32[]{:T(128)S(6)} %add.100, s32[]{:T(128)S(6)} %select_n.18), kind=kOutput, calls=%fused_computation.10 | convolution fusion | flops 4196352000 | bytes 21528584 | tf_op jit(solution)/shard_map/sjmc,scr->jsmr/dot_general | solution.py:112
  590.7 50.3 %reduce-scatter.5.cloned.1.call-done = bf16[1,2640,256]{2,1,0:T(8,128)(2,1)} async-done(((bf16[4,2640,256]{2,1,0:T(8,128)(2,1)}), bf16[1,2640,256]{2,1,0:T(8,128)(2,1)}) %reduce-scatter.5.cloned.1.call-update) | async-done | bytes 1351696 | tf_op jit(solution)/shard_map/reduce_scatter | solution.py:116
  652.4 41.5 %all-gather.3.cloned.1.call-done = bf16[2703360]{0:T(1024)(128)(2,1)} async-done(((bf16[675840]{0:T(1024)(128)(2,1)}), bf16[2703360]{0:T(1024)(128)(2,1)}) %all-gather.3.cloned.1.call-update) | async-done | bytes 5406736 | tf_op jit(solution)/shard_map/all_gather | solution.py:122
  693.9 7.0 reshape.109
  706.9 6.1 broadcast_multiply_fusion
  713.0 14.3 %convolution_multiply_fusion = f32[2,4,1000,1024]{3,2,1,0:T(8,128)} fusion(bf16[4,2,1000,256]{3,2,1,0:T(8,128)(2,1)S(1)} %bitcast.109, bf16[10,2048,256]{2,1,0:T(8,128)(2,1)} %copy-done.7, s32[]{:T(128)S(6)} %add.100, s32[]{:T(128)S(6)} %select_n.18), kind=kOutput, calls=%fused_computation.2 | convolution fusion | flops 4202496000 | bytes 37912584 | tf_op jit(solution)/shard_map/jsmr,scr->sjmc/dot_general | solution.py:127
  729.9 7.2 fusion.1
  737.1 22.5 %fusion = bf16[2,4000,1024]{2,1,0:T(8,128)(2,1)} fusion(f32[2,4,1000,1024]{3,2,1,0:T(8,128)} %convolution_multiply_fusion, bf16[2,4000,1024]{2,1,0:T(8,128)(2,1)} %param.25), kind=kLoop, calls=%fused_computation.1 | loop fusion | flops 32768000 | bytes 65536000 | tf_op jit(solution)/shard_map/convert_element_type | solution.py:129
  (135 shorter events, 86.0 us)
Async XLA Ops:
  7.2 128.3 %all-reduce.6.cloned.1.call-start = ((), (), s32[]{:S(2)}) async-start(), calls=%async_computation.6 | async-start | bytes 10813440 | tf_op jit(solution)/shard_map/psum | solution.py:85
  27.0 249.4 %reduce-scatter.7.cloned.1.call-start = ((), (), s32[]{:S(2)}) async-start(), calls=%async_computation.5 | async-start | bytes 5898240
  135.5 11.6 %copy-start.5 = (bf16[4,128,1024]{2,1,0:T(8,128)(2,1)S(1)}, bf16[4,128,1024]{2,1,0:T(8,128)(2,1)}, u32[]{:S(2)}) copy-start(bf16[4,128,1024]{2,1,0:T(8,128)(2,1)} %param.21) | copy-start | bytes 3145732
  135.5 11.6 %copy-start.22 = (bf16[4,128,256]{2,1,0:T(8,128)(2,1)S(1)}, bf16[4,128,256]{2,1,0:T(8,128)(2,1)}, u32[]{:S(2)}) copy-start(bf16[4,128,256]{2,1,0:T(8,128)(2,1)} %get-tuple-element.10) | copy-start | bytes 786436
  135.5 12.4 %copy-start.3 = (bf16[4,512,1024]{2,1,0:T(8,128)(2,1)S(1)}, bf16[4,512,1024]{2,1,0:T(8,128)(2,1)}, u32[]{:S(2)}) copy-start(bf16[4,512,1024]{2,1,0:T(8,128)(2,1)} %param.16) | copy-start | bytes 12582916
  173.5 245.9 %all-reduce.4.cloned.1.call-start = ((), (), s32[]{:S(2)}) async-start(), calls=%async_computation.2 | async-start | bytes 5242880 | tf_op jit(solution)/shard_map/psum | solution.py:92
  280.8 360.2 %reduce-scatter.5.cloned.1.call-start = ((), (), s32[]{:S(2)}) async-start(), calls=%async_computation.3 | async-start | bytes 6758400 | tf_op jit(solution)/shard_map/reduce_scatter | solution.py:116
  456.0 17.7 %collective-permute-start = (bf16[10,128,256]{2,1,0:T(8,128)(2,1)S(1)}, bf16[10,128,256]{2,1,0:T(8,128)(2,1)S(1)}, u32[]{:S(2)}, u32[]{:S(2)}) collective-permute-start(bf16[10,128,256]{2,1,0:T(8,128)(2,1)S(1)} %convolution_convert_fusion.3), channel_id=1, source_target_pairs={{0,4},{4,8},{8,12},{12,16},{16,20},{20,24},{24,28},{28,0},{1,5},{5... | collective-permute-start | bytes 1966088 | tf_op jit(solution)/shard_map/ppermute | solution.py:98
  473.7 16.7 %collective-permute-start.1 = (bf16[10,128,256]{2,1,0:T(8,128)(2,1)S(1)}, bf16[10,128,256]{2,1,0:T(8,128)(2,1)S(1)}, u32[]{:S(2)}, u32[]{:S(2)}) collective-permute-start(bf16[10,128,256]{2,1,0:T(8,128)(2,1)S(1)} %collective-permute-done), channel_id=1, source_target_pairs={{0,4},{4,8},{8,12},{12,16},{16,20},{20,24},{24,28},{28,0},{1,5},{5... | collective-permute-start | bytes 1966088 | tf_op jit(solution)/shard_map/ppermute | solution.py:98
  491.2 15.8 %collective-permute-start.2 = (bf16[10,128,256]{2,1,0:T(8,128)(2,1)S(1)}, bf16[10,128,256]{2,1,0:T(8,128)(2,1)S(1)}, u32[]{:S(2)}, u32[]{:S(2)}) collective-permute-start(bf16[10,128,256]{2,1,0:T(8,128)(2,1)S(1)} %collective-permute-done.1), channel_id=1, source_target_pairs={{0,4},{4,8},{8,12},{12,16},{16,20},{20,24},{24,28},{28,0},{1,5},{5... | collective-permute-start | bytes 1966088 | tf_op jit(solution)/shard_map/ppermute | solution.py:98
  507.8 14.8 %collective-permute-start.3 = (bf16[10,128,256]{2,1,0:T(8,128)(2,1)S(1)}, bf16[10,128,256]{2,1,0:T(8,128)(2,1)S(1)}, u32[]{:S(2)}, u32[]{:S(2)}) collective-permute-start(bf16[10,128,256]{2,1,0:T(8,128)(2,1)S(1)} %collective-permute-done.2), channel_id=1, source_target_pairs={{0,4},{4,8},{8,12},{12,16},{16,20},{20,24},{24,28},{28,0},{1,5},{5... | collective-permute-start | bytes 1966088 | tf_op jit(solution)/shard_map/ppermute | solution.py:98
  523.5 14.1 %collective-permute-start.4 = (bf16[10,128,256]{2,1,0:T(8,128)(2,1)S(1)}, bf16[10,128,256]{2,1,0:T(8,128)(2,1)S(1)}, u32[]{:S(2)}, u32[]{:S(2)}) collective-permute-start(bf16[10,128,256]{2,1,0:T(8,128)(2,1)S(1)} %collective-permute-done.3), channel_id=1, source_target_pairs={{0,4},{4,8},{8,12},{12,16},{16,20},{20,24},{24,28},{28,0},{1,5},{5... | collective-permute-start | bytes 1966088 | tf_op jit(solution)/shard_map/ppermute | solution.py:98
  538.4 14.9 %collective-permute-start.5 = (bf16[10,128,256]{2,1,0:T(8,128)(2,1)S(1)}, bf16[10,128,256]{2,1,0:T(8,128)(2,1)}, u32[]{:S(2)}, u32[]{:S(2)}) collective-permute-start(bf16[10,128,256]{2,1,0:T(8,128)(2,1)S(1)} %collective-permute-done.4), channel_id=1, source_target_pairs={{0,4},{4,8},{8,12},{12,16},{16,20},{20,24},{24,28},{28,0},{1,5},{5... | collective-permute-start | bytes 1966088 | tf_op jit(solution)/shard_map/ppermute | solution.py:98
  553.3 13.8 %collective-permute-start.6 = (bf16[10,128,256]{2,1,0:T(8,128)(2,1)}, bf16[10,128,256]{2,1,0:T(8,128)(2,1)}, u32[]{:S(2)}, u32[]{:S(2)}) collective-permute-start(bf16[10,128,256]{2,1,0:T(8,128)(2,1)} %collective-permute-done.5), channel_id=1, source_target_pairs={{0,4},{4,8},{8,12},{12,16},{16,20},{20,24},{24,28},{28,0},{1,5},{5... | collective-permute-start | bytes 1966088 | tf_op jit(solution)/shard_map/ppermute | solution.py:98
  553.5 15.9 %copy-start.15 = (bf16[10,128,256]{2,1,0:T(8,128)(2,1)S(1)}, bf16[10,128,256]{2,1,0:T(8,128)(2,1)}, u32[]{:S(2)}) copy-start(bf16[10,128,256]{2,1,0:T(8,128)(2,1)} %copy-done.14) | copy-start | bytes 1966084
  553.5 16.0 %copy-start.13 = (bf16[10,128,256]{2,1,0:T(8,128)(2,1)S(1)}, bf16[10,128,256]{2,1,0:T(8,128)(2,1)}, u32[]{:S(2)}) copy-start(bf16[10,128,256]{2,1,0:T(8,128)(2,1)} %copy-done.12) | copy-start | bytes 1966084
  553.6 16.0 %copy-start.11 = (bf16[10,128,256]{2,1,0:T(8,128)(2,1)S(1)}, bf16[10,128,256]{2,1,0:T(8,128)(2,1)}, u32[]{:S(2)}) copy-start(bf16[10,128,256]{2,1,0:T(8,128)(2,1)} %copy-done.10) | copy-start | bytes 1966084
  590.2 51.7 %copy-start.23 = (f32[4,32,256]{2,1,0:T(8,128)S(1)}, f32[4,32,256]{2,1,0:T(8,128)}, u32[]{:S(2)}) copy-start(f32[4,32,256]{2,1,0:T(8,128)} %param.22) | copy-start | bytes 393220
  590.2 51.7 %copy-start.24 = (f32[4,32,256]{2,1,0:T(8,128)S(1)}, f32[4,32,256]{2,1,0:T(8,128)}, u32[]{:S(2)}) copy-start(f32[4,32,256]{2,1,0:T(8,128)} %param.23) | copy-start | bytes 393220
  590.2 53.6 %copy-start.20 = (f32[4,128,256]{2,1,0:T(8,128)S(1)}, f32[4,128,256]{2,1,0:T(8,128)}, u32[]{:S(2)}) copy-start(f32[4,128,256]{2,1,0:T(8,128)} %param.17) | copy-start | bytes 1572868
  590.2 53.6 %copy-start.21 = (f32[4,128,256]{2,1,0:T(8,128)S(1)}, f32[4,128,256]{2,1,0:T(8,128)}, u32[]{:S(2)}) copy-start(f32[4,128,256]{2,1,0:T(8,128)} %param.18) | copy-start | bytes 1572868
  590.2 103.7 %all-gather.3.cloned.1.call-start = ((), (), s32[]{:S(2)}) async-start(), calls=%async_computation.4 | async-start | bytes 6758400 | tf_op jit(solution)/shard_map/all_gather | solution.py:122
  713.0 14.3 %copy-start.19 = (bf16[4,128,1024]{2,1,0:T(8,128)(2,1)S(1)}, bf16[4,128,1024]{2,1,0:T(8,128)(2,1)}, u32[]{:S(2)}) copy-start(bf16[4,128,1024]{2,1,0:T(8,128)(2,1)} %param.20) | copy-start | bytes 3145732
  737.1 22.5 %copy-start.1 = (bf16[4,1024,256]{2,1,0:T(8,128)(2,1)S(1)}, bf16[4,1024,256]{2,1,0:T(8,128)(2,1)}, u32[]{:S(2)}) copy-start(bf16[4,1024,256]{2,1,0:T(8,128)(2,1)} %param.19) | copy-start | bytes 6291460
  (18 other events, 41.5 us)
Sparse Core Ops, SparseCore 0:
  27.2 108.2 all-reduce.5
  173.6 102.8 reduce-scatter.6
  283.4 135.8 all-reduce.3
  590.3 50.6 reduce-scatter.4
  652.5 41.3 all-gather.2
